TPU v7x, 128 devices: a whole 4x4x4 slice. The times are simulated.
128 devices in a mesh: row: 64 (over z, y, x), col: 2 (over core).
Axes of the slice: x: 4, y: 4, z: 4, core: 2. Of those that a mesh axis runs over, the one named last changes fastest.
Arguments:
- rhs: float32 [2, 64, 1024, 1024], P(None, 'row', None, 'col'), may hold values from -8 to 8
- panels: float32 [2, 2, 64, 1024, 1024], P(None, None, 'row', None, 'col'), may hold values from -0.1875 to 0.1875
- inverses: float32 [2, 1024, 1024], replicated, may hold values from -1 to 4, as said below
Outputs:
- result: float32 [2, 64, 1024, 1024], P(None, 'row', None, 'col')
Inputs may be any that keep to these rules, and one draw needn't show every extreme that they name: Each inverses[k] is lower triangular with a positive diagonal.
All inputs are finite; a program needn't handle non-finite values.
Results may differ from a plain program's by a relative error of at most 0.000075.
Values sent between devices are 32-bit elements; how exact they have to be, the bound alone decides.
No kernel may reach another device: no remote copies, remote signals or barrier semaphores. Data moves between devices by JAX's collectives and lax.ppermute only.
A program may use at most 128 MiB of HBM per device.

v0:
```python
import jax
import jax.numpy as jnp
from jax import lax
from jax.sharding import PartitionSpec as P


def per_device(rhs, panels, inverses):
    highest = lax.Precision.HIGH
    high = highest
    row_index = lax.axis_index("row")
    row_count = lax.axis_size("row")
    col_index = lax.axis_index("col")
    slot_count = rhs.shape[0]
    half = panels.shape[-1]
    block_ids = (jnp.arange(slot_count, dtype=jnp.int32) * row_count + row_index)[
        :, None, None, None
    ]
    swap = [(0, 1), (1, 0)]

    def dot(a, b):
        return jnp.dot(a, b, precision=highest, preferred_element_type=jnp.float32)

    other_panels = lax.ppermute(panels, "col", swap)

    wanted = jnp.stack([rhs[0, 0], rhs[0, 0], panels[0, 0, 0]])
    owner = jnp.array([0, 1, 1], dtype=jnp.int32)[:, None, None]
    spread = lax.psum(jnp.where(owner == row_index, wanted, 0).astype(wanted.dtype), "row")
    rhs0, rhs1, tile_mine = spread[0], spread[1], spread[2]
    tile_other = lax.ppermute(tile_mine, "col", swap)

    def rows_of(solved, which):
        return lax.dynamic_slice_in_dim(solved, which * half, half, axis=0)

    def split_product(mine, other, solved, spec, precision):
        a = jnp.einsum(spec, mine, rows_of(solved, col_index), precision=precision,
                       preferred_element_type=jnp.float32)
        b = jnp.einsum(spec, other, rows_of(solved, 1 - col_index), precision=precision,
                       preferred_element_type=jnp.float32)
        return a + b

    panel_spec = "sqin,nr->sqir"
    solved0 = dot(inverses[0], rhs0)
    sectioned = rhs - split_product(panels[0], other_panels[0], solved0, panel_spec, high)
    sectioned = jnp.where(block_ids >= 1, sectioned, solved0)
    solved1 = dot(inverses[1], rhs1 - split_product(tile_mine, tile_other, solved0, "in,nr->ir", highest))
    updated = sectioned - split_product(panels[1], other_panels[1], solved1, panel_spec, high)
    return jnp.where(block_ids >= 2, updated, jnp.where(block_ids == 1, solved1, sectioned))


def solution(mesh):
    placed = (P(None, "row", None, "col"), P(None, None, "row", None, "col"), P())
    return jax.shard_map(
        per_device,
        mesh=mesh,
        in_specs=placed,
        out_specs=P(None, "row", None, "col"),
        check_vma=False,
    )
```

profile of v0, /device:TPU:1, one launch (start us, length us, event | category | flops | bytes accessed | tf_op | source)
XLA Modules:
  0.0 237.2 jit_solution(2126987660787302311)
XLA Ops:
  6.5 0.0 all-reduce.2.cloned.1.call-start
  6.5 0.0 copy-start
  6.5 1.8 slice_bitcast_fusion.15
  8.3 1.8 slice_bitcast_fusion.14
  10.1 0.0 copy-done
  10.1 3.5 %maximum_select_fusion = f32[3,1024,512]{2,1,0:T(8,128)} fusion(f32[1,1024,512]{2,1,0:T(8,128)S(1)} %slice_bitcast_fusion.14, f32[1,1024,512]{2,1,0:T(8,128)S(1)} %slice_bitcast_fusion.15, pred[3]{0:T(512)(128)(4,1)S(1)} %broadcast_compare_fusion), kind=kLoop, calls=%fused_computation | loop fusion | flops 4718592 | bytes 10485763 | tf_op jit(solution)/shard_map/jit(_where)/select_n | solution.py:27
  13.6 0.0 all-reduce.2.cloned.1.call-update
  13.6 1.5 collective-permute-start
  15.1 149.1 %all-reduce.2.cloned.1.call-done = f32[3,1024,512]{2,1,0:T(8,128)} async-done(((f32[3,1024,512]{2,1,0:T(8,128)}), f32[3,1024,512]{2,1,0:T(8,128)}) %all-reduce.2.cloned.1.call-update) | async-done | bytes 6291472 | tf_op jit(solution)/shard_map/psum | solution.py:27
  164.3 3.1 %slice_bitcast_fusion.10 = f32[1024,512]{1,0:T(8,128)} fusion(f32[3,1024,512]{2,1,0:T(8,128)} %all-reduce.2.cloned.1.call-done), kind=kLoop, calls=%fused_computation.19 | loop fusion | bytes 4194304 | tf_op jit(solution)/shard_map/squeeze | solution.py:28
  167.3 1.1 collective-permute-start.1
  168.5 5.3 %copy.7 = f32[2,1,1024,512]{2,3,0,1:T(8,128)} copy(f32[2,1,1024,512]{3,2,1,0:T(8,128)} %param.4) | data formatting | bytes 8388608 | tf_op args[0]
  173.8 9.4 %fusion.8 = f32[512,1024]{1,0:T(8,128)S(1)} fusion(f32[2,1024,1024]{2,1,0:T(8,128)} %param.6, f32[3,1024,512]{2,1,0:T(8,128)} %all-reduce.2.cloned.1.call-done), kind=kOutput, calls=%fused_computation.15 | convolution fusion | flops 3221225472 | bytes 8388608 | tf_op jit(solution)/shard_map/dot_general | solution.py:21
  183.2 0.0 slice-start.2
  183.2 3.6 %fusion.24 = f32[1024,512]{1,0:T(8,128)S(1)} fusion(f32[512,1024]{1,0:T(8,128)S(1)} %fusion.8, s32[]{:T(128)S(6)} %select_n.27, f32[3,1024,512]{2,1,0:T(8,128)} %all-reduce.2.cloned.1.call-done), kind=kOutput, calls=%fused_computation.35 | convolution fusion | flops 1610612736 | bytes 5242884 | tf_op jit(solution)/shard_map/in,nr->ir/dot_general | solution.py:35
  186.9 0.0 slice-start.3
  186.9 6.4 %fusion.3 = f32[512,2,1024]{2,0,1:T(8,128)S(1)} fusion(f32[2,2,1,1024,512]{4,3,1,2,0:T(8,128)} %bitcast.70, f32[512,1024]{1,0:T(8,128)S(1)} %fusion.8, s32[]{:T(128)S(6)} %select_n.27), kind=kOutput, calls=%fused_computation.8 | convolution fusion | flops 3221225472 | bytes 9437188 | tf_op jit(solution)/shard_map/sqin,nr->sqir/dot_general | solution.py:35
  193.3 0.0 collective-permute-done.1
  193.3 0.0 slice-start
  193.4 1.9 fusion.21
  195.2 0.0 slice-done.2
  195.2 0.0 slice-done.3
  195.3 0.0 slice-start.1
  195.3 8.5 %fusion.6 = f32[512,1024]{1,0:T(8,128)S(1)} fusion(f32[2,1024,1024]{2,1,0:T(8,128)S(1)} %bitcast.75, f32[3,1024,512]{2,1,0:T(8,128)} %all-reduce.2.cloned.1.call-done, f32[1024,512]{1,0:T(8,128)S(1)} %fusion.24, f32[1024,512]{1,0:T(8,128)S(1)} %fusion.21), kind=kOutput, calls=%fused_computation.13 | convolution fusion | flops 3222274048 | bytes 12582912 | tf_op jit(solution)/shard_map/dot_general | solution.py:21
  203.8 0.0 slice-done
  203.8 0.0 slice-done.1
  203.8 3.9 %fusion.1 = f32[512,2,1024]{2,0,1:T(8,128)S(1)} fusion(f32[2,2,1,1024,512]{4,3,1,2,0:T(8,128)S(1)} %bitcast.73, f32[512,1024]{1,0:T(8,128)S(1)} %fusion.6, s32[]{:T(128)S(6)} %select_n.27), kind=kOutput, calls=%fused_computation.4 | convolution fusion | flops 3221225472 | bytes 9437188 | tf_op jit(solution)/shard_map/sqin,nr->sqir/dot_general | solution.py:35
  207.8 0.0 collective-permute-done
  207.8 7.3 %fusion.2 = f32[512,2,1024]{2,0,1:T(8,128)} fusion(f32[2,2,1,1024,512]{4,3,1,2,0:T(8,128)} %collective-permute-done, f32[512,1024]{1,0:T(8,128)S(1)} %fusion.8, s32[]{:T(128)S(6)} %select_n.28), kind=kOutput, calls=%fused_computation.6 | convolution fusion | flops 3221225472 | bytes 9437188 | tf_op jit(solution)/shard_map/sqin,nr->sqir/dot_general | solution.py:37
  215.1 9.9 %fusion.4 = f32[2,1,1024,512]{2,3,0,1:T(8,128)} fusion(f32[2,1,1024,512]{2,3,0,1:T(8,128)} %copy.7, f32[512,2,1024]{2,0,1:T(8,128)S(1)} %fusion.1, f32[512,2,1024]{2,0,1:T(8,128)S(1)} %fusion.3, f32[512,2,1024]{2,0,1:T(8,128)} %fusion.2, f32[2,2,1,1024,512]{4,3,1,2,0:T(8,128)} %collective-permute-done, f32[1024,512]{0,1:T(8,128)S(1)} %bitcast.68, ...), kind=kOutput, calls=%fused_computation.10 | convolution fusion | flops 3228565504 | bytes 30410244 | tf_op jit(solution)/shard_map/sqin,nr->sqir/dot_general | solution.py:37
  225.0 5.4 %copy.9 = f32[2,1,1024,512]{3,2,1,0:T(8,128)} copy(f32[2,1,1024,512]{2,3,0,1:T(8,128)} %fusion.4) | data formatting | bytes 8388608 | tf_op jit(solution)/shard_map/jit(_where)/select_n | solution.py:47
  (5 shorter events, 0.0 us)
Async XLA Ops:
  6.5 157.7 %all-reduce.2.cloned.1.call-start = ((), (), s32[]{:S(2)}) async-start(), calls=%async_computation | async-start | bytes 12582912 | tf_op jit(solution)/shard_map/psum | solution.py:27
  6.5 3.5 %copy-start = (s32[3]{0:T(128)S(1)}, s32[3]{0:T(128)}, u32[]{:S(2)}) copy-start(s32[3]{0:T(128)} %constant.25.clone) | copy-start | bytes 40
  13.6 194.1 %collective-permute-start = (f32[2,2,1,1024,512]{4,3,1,2,0:T(8,128)}, f32[2,2,1,1024,512]{4,3,1,2,0:T(8,128)}, u32[]{:S(2)}, u32[]{:S(2)}) collective-permute-start(f32[2,2,1,1024,512]{4,3,1,2,0:T(8,128)} %bitcast.69), channel_id=1, source_target_pairs={{0,1},{1,0},{2,3},{3,2},{4,5},{5,4},{6,7},{7,6},{8,9},{9,8},{10,11... | collective-permute-start | bytes 25165832 | tf_op jit(solution)/shard_map/ppermute | solution.py:23
  167.3 26.0 %collective-permute-start.1 = (f32[1024,512]{1,0:T(8,128)}, f32[1024,512]{1,0:T(8,128)S(1)}, u32[]{:S(2)}, u32[]{:S(2)}) collective-permute-start(f32[1024,512]{1,0:T(8,128)} %slice_bitcast_fusion.10), channel_id=1, source_target_pairs={{0,1},{1,0},{2,3},{3,2},{4,5},{5,4},{6,7},{7,6},{8,9},{9,8},{10,11... | collective-permute-start | bytes 6291464 | tf_op jit(solution)/shard_map/ppermute | solution.py:29
  183.2 12.0 %slice-start.2 = ((s8[8388608]{0:T(1024)(128)(4,1)}), s8[4194304]{0:T(1024)(128)(4,1)S(1)}, s32[]{:S(2)}) async-start(s8[8388608]{0:T(1024)(128)(4,1)} %bitcast.74), calls=%async_computation.3 | async-start | bytes 8388608
  186.9 8.4 %slice-start.3 = ((s8[8388608]{0:T(1024)(128)(4,1)}), s8[4194304]{0:T(1024)(128)(4,1)S(1)}, s32[]{:S(2)}) async-start(s8[8388608]{0:T(1024)(128)(4,1)} %bitcast.74), calls=%async_computation.4 | async-start | bytes 8388608
  193.3 10.4 %slice-start = ((s8[8388608]{0:T(1024)(128)(4,1)}), s8[4194304]{0:T(1024)(128)(4,1)S(1)}, s32[]{:S(2)}) async-start(s8[8388608]{0:T(1024)(128)(4,1)} %bitcast.71), calls=%async_computation.1 | async-start | bytes 8388608
  195.3 8.5 %slice-start.1 = ((s8[8388608]{0:T(1024)(128)(4,1)}), s8[4194304]{0:T(1024)(128)(4,1)S(1)}, s32[]{:S(2)}) async-start(s8[8388608]{0:T(1024)(128)(4,1)} %bitcast.71), calls=%async_computation.2 | async-start | bytes 8388608
Sparse Core Ops, SparseCore 0:
  13.7 150.4 all-reduce.1
where the time goes:
time: 238 us; the launch traced here: 237 us
  waiting for transfers between devices  149 us (63%)
  matrix products  51 us (21%)
  local copies, waits for them, and re-layouts  17.3 us (7%)
  between operations  13.6 us (6%)
  other arithmetic  3.51 us (1%)
  starting transfers between devices  2.65 us (1%)
    psum x1, waiting for transfers between devices, per_device(): lax.psum(jnp.where(owner == row_index, wanted, 0).astype(wanted.dtype), '...  149 us
    dot_general x3, matrix products, split_product(): jnp.einsum(spec, other, rows_of(solved, 1 - col_index), precision=precisi...  19.1 us
    dot_general x2, matrix products, dot(): return jnp.dot(a, b, precision=highest, preferred_element_type=jnp.float32)  17.9 us
    dot_general x3, matrix products, split_product(): jnp.einsum(spec, mine, rows_of(solved, col_index), precision=precision, p...  14 us
    unnamed x11, local copies, waits for them, and re-layouts  5.38 us
    select_n x1, local copies, waits for them, and re-layouts, per_device(): jnp.where(block_ids >= 2, updated, jnp.where(block_ids == 1, solved1, sec...  5.36 us
  transfers between devices with their start and end apart: 3, of which 1 were waited for; matrix products, arithmetic and copies ran while one was open for 18% of the time, Pallas kernels for 0%

commit v1 on v0

--- a/solution.py
+++ b/solution.py
@@ -20,6 +20,11 @@
     def dot(a, b):
         return jnp.dot(a, b, precision=highest, preferred_element_type=jnp.float32)
 
+    def lower_dot(lower, b):
+        h = lower.shape[0] // 2
+        top = dot(lower[:h, :h], b[:h])
+        return jnp.concatenate([top, dot(lower[h:], b)], axis=0)
+
     other_panels = lax.ppermute(panels, "col", swap)
 
     wanted = jnp.stack([rhs[0, 0], rhs[0, 0], panels[0, 0, 0]])
@@ -39,10 +44,10 @@
         return a + b
 
     panel_spec = "sqin,nr->sqir"
-    solved0 = dot(inverses[0], rhs0)
+    solved0 = lower_dot(inverses[0], rhs0)
     sectioned = rhs - split_product(panels[0], other_panels[0], solved0, panel_spec, high)
     sectioned = jnp.where(block_ids >= 1, sectioned, solved0)
-    solved1 = dot(inverses[1], rhs1 - split_product(tile_mine, tile_other, solved0, "in,nr->ir", highest))
+    solved1 = lower_dot(inverses[1], rhs1 - split_product(tile_mine, tile_other, solved0, "in,nr->ir", highest))
     updated = sectioned - split_product(panels[1], other_panels[1], solved1, panel_spec, high)
     return jnp.where(block_ids >= 2, updated, jnp.where(block_ids == 1, solved1, sectioned))
 

time: 238 us -> 263 us (1.11)
  matrix products: 51 us -> 65.2 us
  local copies, waits for them, and re-layouts: 17.3 us -> 30.6 us
  waiting for transfers between devices: 149 us -> 144 us
  other arithmetic: 3.51 us -> 6.53 us
    dot_general x3, matrix products: 14 us -> 25.6 us  [split_product(): jnp.einsum(spec, mine, rows_of(solved, col_index), precision=precision, p...]
    dot_general x3, matrix products: 19.1 us -> 29.4 us  [split_product(): jnp.einsum(spec, other, rows_of(solved, 1 - col_index), precision=precisi...]
    dot_general x2 -> x4, matrix products: 17.9 us -> 10.1 us  [dot(): return jnp.dot(a, b, precision=highest, preferred_element_type=jnp.float32)]
    squeeze x0 -> x1, local copies, waits for them, and re-layouts: none -> 6.75 us  [per_device(): solved0 = lower_dot(inverses[0], rhs0)]
    concatenate x0 -> x2, local copies, waits for them, and re-layouts: none -> 5.83 us  [lower_dot(): return jnp.concatenate([top, dot(lower[h:], b)], axis=0)]
    psum x1, waiting for transfers between devices: 149 us -> 144 us  [per_device(): lax.psum(jnp.where(owner == row_index, wanted, 0).astype(wanted.dtype), '...]
    concatenate x0 -> x2, other arithmetic: none -> 3.01 us  [lower_dot(): return jnp.concatenate([top, dot(lower[h:], b)], axis=0)]
    unnamed x11 -> x19, local copies, waits for them, and re-layouts: 5.38 us -> 7.32 us
  transfers between devices with their start and end apart: 3 -> 3, of which waited for: 1 -> 1; matrix products, arithmetic and copies ran while one was open for 18% -> 24% of each run, Pallas kernels for 0% -> 0%
where the time goes in v1:
time: 263 us; the launch traced here: 262 us
  waiting for transfers between devices  144 us (55%)
  matrix products  65.2 us (25%)
  local copies, waits for them, and re-layouts  30.6 us (12%)
  between operations  13.5 us (5%)
  other arithmetic  6.53 us (2%)
  starting transfers between devices  2.65 us (1%)
    psum x1, waiting for transfers between devices, per_device(): lax.psum(jnp.where(owner == row_index, wanted, 0).astype(wanted.dtype), '...  144 us
    dot_general x3, matrix products, split_product(): jnp.einsum(spec, other, rows_of(solved, 1 - col_index), precision=precisi...  29.4 us
    dot_general x3, matrix products, split_product(): jnp.einsum(spec, mine, rows_of(solved, col_index), precision=precision, p...  25.6 us
    dot_general x4, matrix products, dot(): return jnp.dot(a, b, precision=highest, preferred_element_type=jnp.float32)  10.1 us
    unnamed x19, local copies, waits for them, and re-layouts  7.32 us
    squeeze x1, local copies, waits for them, and re-layouts, per_device(): solved0 = lower_dot(inverses[0], rhs0)  6.75 us
    concatenate x2, local copies, waits for them, and re-layouts, lower_dot(): return jnp.concatenate([top, dot(lower[h:], b)], axis=0)  5.83 us
    select_n x1, local copies, waits for them, and re-layouts, per_device(): jnp.where(block_ids >= 2, updated, jnp.where(block_ids == 1, solved1, sec...  5.36 us
  transfers between devices with their start and end apart: 3, of which 1 were waited for; matrix products, arithmetic and copies ran while one was open for 24% of the time, Pallas kernels for 0%

profile of v1, /device:TPU:1, one launch (start us, length us, event | category | flops | bytes accessed | tf_op | source)
XLA Modules:
  0.0 262.2 jit_solution(1259263313795949196)
XLA Ops:
  6.5 0.0 all-reduce.2.cloned.1.call-start
  6.5 0.0 copy-start.5
  6.5 0.0 copy-start.6
  6.5 1.9 slice_bitcast_fusion.16
  8.5 0.9 copy-done.5
  9.4 0.2 slice_bitcast_fusion.17
  9.5 0.0 copy-done.6
  9.6 3.5 %maximum_select_fusion = f32[3,1024,512]{2,1,0:T(8,128)} fusion(f32[1,1024,512]{2,1,0:T(8,128)S(1)} %slice_bitcast_fusion.16, f32[1,1024,512]{2,1,0:T(8,128)S(1)} %slice_bitcast_fusion.17, pred[3]{0:T(512)(128)(4,1)S(1)} %broadcast_compare_fusion), kind=kLoop, calls=%fused_computation | loop fusion | flops 4718592 | bytes 10485763 | tf_op jit(solution)/shard_map/jit(_where)/select_n | solution.py:32
  13.0 0.0 all-reduce.2.cloned.1.call-update
  13.1 1.5 collective-permute-start
  14.6 5.3 %copy.9 = f32[2,1,1024,512]{2,3,0,1:T(8,128)} copy(f32[2,1,1024,512]{3,2,1,0:T(8,128)} %param.4) | data formatting | bytes 8388608 | tf_op args[0]
  19.9 143.8 %all-reduce.2.cloned.1.call-done = f32[3,1024,512]{2,1,0:T(8,128)} async-done(((f32[3,1024,512]{2,1,0:T(8,128)}), f32[3,1024,512]{2,1,0:T(8,128)}) %all-reduce.2.cloned.1.call-update) | async-done | bytes 6291472 | tf_op jit(solution)/shard_map/psum | solution.py:32
  163.7 0.0 slice-start
  163.7 3.2 %slice_bitcast_fusion.12 = f32[1024,512]{1,0:T(8,128)} fusion(f32[3,1024,512]{2,1,0:T(8,128)} %all-reduce.2.cloned.1.call-done), kind=kLoop, calls=%fused_computation.25 | loop fusion | bytes 4194304 | tf_op jit(solution)/shard_map/squeeze | solution.py:33
  166.9 0.0 slice-start.1
  166.9 1.1 collective-permute-start.1
  168.1 6.7 %slice_bitcast_fusion.9 = (f32[1024,1024]{1,0:T(8,128)S(1)}, f32[1024,1024]{1,0:T(8,128)}) fusion(f32[2,1024,1024]{2,1,0:T(8,128)} %param.6), kind=kLoop, calls=%fused_computation.14 | loop fusion | bytes 16777216 | tf_op jit(solution)/shard_map/squeeze | solution.py:47
  174.8 0.0 slice-done
  174.8 0.0 slice-done.1
  174.9 1.0 convolution_bitcast_fusion.1
  175.9 3.4 %fusion.16 = f32[512,512]{1,0:T(8,128)S(1)} fusion(f32[2,1024,1024]{2,1,0:T(8,128)} %param.6, f32[3,1024,512]{2,1,0:T(8,128)S(1)} %bitcast.87), kind=kOutput, calls=%fused_computation.38 | convolution fusion | flops 1610612736 | bytes 5242880 | tf_op jit(solution)/shard_map/dot_general | solution.py:21
  179.3 1.5 pad_maximum_fusion
  180.8 2.9 %copy.10 = f32[1024,512]{0,1:T(8,128)} copy(f32[1024,512]{1,0:T(8,128)} %pad_maximum_fusion) | data formatting | bytes 4194304 | tf_op jit(solution)/shard_map/concatenate | solution.py:26
  183.7 3.5 %fusion.34 = f32[1024,512]{1,0:T(8,128)S(1)} fusion(s32[]{:T(128)S(6)} %select_n.27, f32[512,512]{1,0:T(8,128)S(1)} %convolution_bitcast_fusion.1, f32[512,512]{1,0:T(8,128)S(1)} %fusion.16, f32[3,1024,512]{2,1,0:T(8,128)} %all-reduce.2.cloned.1.call-done), kind=kOutput, calls=%fused_computation.53 | convolution fusion | flops 1610874880 | bytes 6291460 | tf_op jit(solution)/shard_map/in,nr->ir/dot_general | solution.py:40
  187.2 10.7 %fusion.3 = f32[512,2,1024]{2,0,1:T(8,128)} fusion(f32[2,2,1,1024,512]{4,3,1,2,0:T(8,128)} %bitcast.89, s32[]{:T(128)S(6)} %select_n.27, f32[512,512]{1,0:T(8,128)S(1)} %convolution_bitcast_fusion.1, f32[512,512]{1,0:T(8,128)S(1)} %fusion.16), kind=kOutput, calls=%fused_computation.8 | convolution fusion | flops 3221487616 | bytes 10485764 | tf_op jit(solution)/shard_map/sqin,nr->sqir/dot_general | solution.py:40
  197.9 0.0 collective-permute-done.1
  197.9 4.3 %fusion.6 = f32[1024,512]{1,0:T(8,128)S(1)} fusion(f32[3,1024,512]{2,1,0:T(8,128)} %all-reduce.2.cloned.1.call-done, f32[1024,512]{1,0:T(8,128)S(1)} %fusion.34, f32[1024,512]{1,0:T(8,128)} %collective-permute-done.1, s32[]{:T(128)S(6)} %select_n.28, f32[512,512]{1,0:T(8,128)S(1)} %convolution_bitcast_fusion.1, f32[512,512]{1,0:T(8,128)S(1)} %fusion.16), kind=kOutput, calls=%fused_computation.27 | convolution fusion | flops 1611923456 | bytes 10485764 | tf_op jit(solution)/shard_map/in,nr->ir/dot_general | solution.py:42
  202.2 2.2 convolution_bitcast_fusion
  204.5 3.4 %fusion.13 = f32[512,512]{1,0:T(8,128)S(1)} fusion(f32[1024,512]{1,0:T(8,128)S(1)} %fusion.6, f32[2,1024,1024]{2,1,0:T(8,128)} %param.6), kind=kOutput, calls=%fused_computation.37 | convolution fusion | flops 1610612736 | bytes 5242880 | tf_op jit(solution)/shard_map/dot_general | solution.py:21
  207.9 0.0 copy-start.4
  207.9 1.1 copy-done.4
  209.0 1.5 pad_maximum_fusion.1
  210.5 2.9 %copy.14 = f32[1024,512]{0,1:T(8,128)} copy(f32[1024,512]{1,0:T(8,128)} %pad_maximum_fusion.1) | data formatting | bytes 4194304 | tf_op jit(solution)/shard_map/concatenate | solution.py:26
  213.4 0.0 copy-start.3
  213.4 11.4 %fusion.1 = f32[512,2,1024]{2,0,1:T(8,128)} fusion(f32[2,2,1,1024,512]{4,3,1,2,0:T(8,128)} %bitcast.90, s32[]{:T(128)S(6)} %select_n.27, f32[512,512]{1,0:T(8,128)S(1)} %convolution_bitcast_fusion, f32[512,512]{1,0:T(8,128)} %copy-done.4), kind=kOutput, calls=%fused_computation.4 | convolution fusion | flops 3221487616 | bytes 10485764 | tf_op jit(solution)/shard_map/sqin,nr->sqir/dot_general | solution.py:40
  224.8 0.0 copy-start
  224.8 0.0 copy-start.1
  224.9 0.0 copy-start.2
  224.9 0.0 collective-permute-done
  224.9 10.8 %fusion.2 = f32[512,2,1024]{2,0,1:T(8,128)} fusion(f32[2,2,1,1024,512]{4,3,1,2,0:T(8,128)} %collective-permute-done, s32[]{:T(128)S(6)} %select_n.28, f32[512,512]{1,0:T(8,128)S(1)} %convolution_bitcast_fusion.1, f32[512,512]{1,0:T(8,128)S(1)} %fusion.16), kind=kOutput, calls=%fused_computation.6 | convolution fusion | flops 3221487616 | bytes 10485764 | tf_op jit(solution)/shard_map/sqin,nr->sqir/dot_general | solution.py:42
  235.7 0.0 copy-done.3
  235.7 0.0 copy-done
  235.7 0.0 copy-done.1
  235.7 0.0 copy-done.2
  235.7 14.3 %fusion.4 = f32[2,1,1024,512]{2,3,0,1:T(8,128)} fusion(f32[2,1,1024,512]{2,3,0,1:T(8,128)S(1)} %copy-done.2, f32[512,2,1024]{2,0,1:T(8,128)} %fusion.1, f32[512,2,1024]{2,0,1:T(8,128)S(1)} %copy-done.3, f32[512,2,1024]{2,0,1:T(8,128)} %fusion.2, f32[2,2,1,1024,512]{4,3,1,2,0:T(8,128)} %collective-permute-done, f32[1024,512]{0,1:T(8,128)S(1)} %copy-done.1, ...), kind=kOutput, calls=%fused_computation.10 | convolution fusion | flops 3228827648 | bytes 31457290 | tf_op jit(solution)/shard_map/sqin,nr->sqir/dot_general | solution.py:42
  250.0 5.4 %copy.15 = f32[2,1,1024,512]{3,2,1,0:T(8,128)} copy(f32[2,1,1024,512]{2,3,0,1:T(8,128)} %fusion.4) | data formatting | bytes 8388608 | tf_op jit(solution)/shard_map/jit(_where)/select_n | solution.py:52
  (4 shorter events, 0.0 us)
Async XLA Ops:
  6.5 157.2 %all-reduce.2.cloned.1.call-start = ((), (), s32[]{:S(2)}) async-start(), calls=%async_computation | async-start | bytes 12582912 | tf_op jit(solution)/shard_map/psum | solution.py:32
  6.5 2.8 %copy-start.5 = (f32[2,1,1024,512]{3,2,1,0:T(8,128)S(1)}, f32[2,1,1024,512]{3,2,1,0:T(8,128)}, u32[]{:S(2)}) copy-start(f32[2,1,1024,512]{3,2,1,0:T(8,128)} %param.4) | copy-start | bytes 12582916
  6.5 3.0 %copy-start.6 = (s32[3]{0:T(128)S(1)}, s32[3]{0:T(128)}, u32[]{:S(2)}) copy-start(s32[3]{0:T(128)} %constant.25.clone) | copy-start | bytes 40
  13.1 211.8 %collective-permute-start = (f32[2,2,1,1024,512]{4,3,1,2,0:T(8,128)}, f32[2,2,1,1024,512]{4,3,1,2,0:T(8,128)}, u32[]{:S(2)}, u32[]{:S(2)}) collective-permute-start(f32[2,2,1,1024,512]{4,3,1,2,0:T(8,128)} %bitcast.88), channel_id=1, source_target_pairs={{0,1},{1,0},{2,3},{3,2},{4,5},{5,4},{6,7},{7,6},{8,9},{9,8},{10,11... | collective-permute-start | bytes 25165832 | tf_op jit(solution)/shard_map/ppermute | solution.py:28
  163.7 11.1 %slice-start = ((s8[6291456]{0:T(1024)(128)(4,1)}), s8[4194304]{0:T(1024)(128)(4,1)S(1)}, s32[]{:S(2)}) async-start(s8[6291456]{0:T(1024)(128)(4,1)} %bitcast.86), calls=%async_computation.1 | async-start | bytes 8388608
  166.9 7.9 %slice-start.1 = ((s8[6291456]{0:T(1024)(128)(4,1)}), s8[2097152]{0:T(1024)(128)(4,1)S(1)}, s32[]{:S(2)}) async-start(s8[6291456]{0:T(1024)(128)(4,1)} %bitcast.86), calls=%async_computation.2 | async-start | bytes 4194304
  166.9 31.0 %collective-permute-start.1 = (f32[1024,512]{1,0:T(8,128)}, f32[1024,512]{1,0:T(8,128)}, u32[]{:S(2)}, u32[]{:S(2)}) collective-permute-start(f32[1024,512]{1,0:T(8,128)} %slice_bitcast_fusion.12), channel_id=1, source_target_pairs={{0,1},{1,0},{2,3},{3,2},{4,5},{5,4},{6,7},{7,6},{8,9},{9,8},{10,11... | collective-permute-start | bytes 6291464 | tf_op jit(solution)/shard_map/ppermute | solution.py:34
  207.9 1.1 copy-start.4
  213.4 22.3 %copy-start.3 = (f32[512,2,1024]{2,0,1:T(8,128)S(1)}, f32[512,2,1024]{2,0,1:T(8,128)}, u32[]{:S(2)}) copy-start(f32[512,2,1024]{2,0,1:T(8,128)} %fusion.3) | copy-start | bytes 12582916
  224.8 10.8 %copy-start = (f32[1024,512]{0,1:T(8,128)S(1)}, f32[1024,512]{0,1:T(8,128)}, u32[]{:S(2)}) copy-start(f32[1024,512]{0,1:T(8,128)} %copy.10) | copy-start | bytes 6291460
  224.8 10.8 %copy-start.1 = (f32[1024,512]{0,1:T(8,128)S(1)}, f32[1024,512]{0,1:T(8,128)}, u32[]{:S(2)}) copy-start(f32[1024,512]{0,1:T(8,128)} %copy.14) | copy-start | bytes 6291460
  224.9 10.8 %copy-start.2 = (f32[2,1,1024,512]{2,3,0,1:T(8,128)S(1)}, f32[2,1,1024,512]{2,3,0,1:T(8,128)}, u32[]{:S(2)}) copy-start(f32[2,1,1024,512]{2,3,0,1:T(8,128)} %copy.9) | copy-start | bytes 12582916
Sparse Core Ops, SparseCore 0:
  13.2 150.4 all-reduce.1
